TPU v7x, 32 devices: a whole 2x2x4 slice. The times are simulated.
32 devices in a mesh: dp: 2 (over y), row: 4 (over x, core), col: 4 (over z).
Axes of the slice: x: 2, y: 2, z: 4, core: 2. Of those that a mesh axis runs over, the one named last changes fastest.
Arguments:
- patches: bfloat16 [2, 512, 1456], P('dp', 'col', 'row'), may hold values from -6 to 6
- queries: bfloat16 [2, 512, 6144], P('dp', 'col', 'row'), may hold values from -6 to 6
- attn_keys: bfloat16 [2, 512, 6144], P('dp', 'col', 'row'), may hold values from -6 to 6
- attn_values: bfloat16 [2, 512, 6144], P('dp', 'col', 'row'), may hold values from -6 to 6
- out_weight: bfloat16 [6144, 12288], P('row', 'col'), may hold values from -0.15625 to 0.15625
- output_grad: bfloat16 [2, 512, 12288], P('dp', 'row', 'col'), may hold values from -4 to 4
Outputs:
- query_grad: float32 [2, 512, 6144], P('dp', 'col', 'row')
- key_grad: float32 [2, 512, 6144], P('dp', 'col', 'row')
- value_grad: float32 [2, 512, 6144], P('dp', 'col', 'row')
- out_weight_grad: float32 [6144, 12288], P('row', 'col')
- embed_weight_grad: float32 [1456, 12288], P('row', 'col')
All inputs are finite; a program needn't handle non-finite values.
Results may differ from a plain program's by a relative error of at most 0.025.
Values may be sent and summed in bfloat16 or wider, within the bound.
No kernel may reach another device: no remote copies, remote signals or barrier semaphores. Data moves between devices by JAX's collectives and lax.ppermute only.
A program may use at most 128 MiB of HBM per device.

v0:
```python
import jax
import jax.numpy as jnp
from jax import lax
from jax.sharding import PartitionSpec as P

DH = 128


def contract_rows(left, right):
    return lax.dot_general(
        left, right, (((0,), (0,)), ((), ())), preferred_element_type=jnp.float32
    )


def body(patches, queries, attn_keys, attn_values, out_weight, output_grad):
    factor = DH ** (-0.5)
    local_rows = queries.shape[1]
    feature_width = queries.shape[2]
    head_count = feature_width // DH
    every_key, every_value, every_patch = (
        lax.all_gather(attn_keys, "col", axis=1, tiled=True),
        lax.all_gather(attn_values, "col", axis=1, tiled=True),
        lax.all_gather(patches, "col", axis=1, tiled=True),
    )
    local_query = queries[0].reshape(local_rows, head_count, DH)
    all_keys = every_key[0].reshape(-1, head_count, DH)
    all_values = every_value[0].reshape(-1, head_count, DH)
    scores = (
        jnp.einsum("qhd,khd->hqk", local_query, all_keys, preferred_element_type=jnp.float32)
        * factor
    )
    row_max = jnp.max(scores, axis=2, keepdims=True)
    log_total = row_max + jnp.log(jnp.sum(jnp.exp(scores - row_max), axis=2, keepdims=True))
    attn_probs = jnp.exp(scores - log_total).astype(jnp.bfloat16)
    attn_out = jnp.einsum(
        "hqk,khd->qhd", attn_probs, all_values, preferred_element_type=jnp.float32
    ).astype(jnp.bfloat16)
    out_local = attn_out.reshape(1, local_rows, feature_width)
    dense_grad = lax.all_gather(output_grad, "row", axis=1, tiled=True)[0]
    attn_grad = lax.psum_scatter(
        lax.dot_general(
            dense_grad, out_weight, (((1,), (1,)), ((), ())), preferred_element_type=jnp.float32
        ),
        "col",
        scatter_dimension=0,
        tiled=True,
    ).astype(jnp.bfloat16)
    grad_heads = attn_grad.reshape(local_rows, head_count, DH)
    prob_grad = jnp.einsum(
        "qhd,khd->hqk", grad_heads, all_values, preferred_element_type=jnp.float32
    )
    row_dot = jnp.transpose(
        jnp.sum(grad_heads.astype(jnp.float32) * attn_out.astype(jnp.float32), axis=2)
    )[:, :, None]
    score_grad = (attn_probs.astype(jnp.float32) * (prob_grad - row_dot)).astype(jnp.bfloat16)
    query_grad = (
        jnp.einsum("hqk,khd->qhd", score_grad, all_keys, preferred_element_type=jnp.float32)
        * factor
    )
    every_out = lax.all_gather(out_local, "col", axis=1, tiled=True)
    key_term = (
        jnp.einsum("hqk,qhd->khd", score_grad, local_query, preferred_element_type=jnp.float32)
        * factor
    )
    value_term = jnp.einsum(
        "hqk,qhd->khd", attn_probs, grad_heads, preferred_element_type=jnp.float32
    )
    key_sum, value_sum = (
        lax.psum_scatter(
            key_term.reshape(-1, feature_width).astype(jnp.bfloat16),
            "col",
            scatter_dimension=0,
            tiled=True,
        ).astype(jnp.float32),
        lax.psum_scatter(
            value_term.reshape(-1, feature_width).astype(jnp.bfloat16),
            "col",
            scatter_dimension=0,
            tiled=True,
        ).astype(jnp.float32),
    )
    out_part = contract_rows(every_out[0], dense_grad)
    embed_part = contract_rows(every_patch[0], dense_grad)
    out_weight_grad, embed_weight_grad = (
        lax.psum(out_part.astype(jnp.bfloat16), "dp").astype(jnp.float32),
        lax.psum(embed_part.astype(jnp.bfloat16), "dp").astype(jnp.float32),
    )
    return (
        query_grad.reshape(1, local_rows, feature_width),
        key_sum.reshape(1, local_rows, feature_width),
        value_sum.reshape(1, local_rows, feature_width),
        out_weight_grad,
        embed_weight_grad,
    )


def solution(mesh):
    placed = (
        P("dp", "col", "row"),
        P("dp", "col", "row"),
        P("dp", "col", "row"),
        P("dp", "col", "row"),
        P("row", "col"),
        P("dp", "row", "col"),
    )
    return jax.shard_map(
        body,
        mesh=mesh,
        in_specs=placed,
        out_specs=(
            P("dp", "col", "row"),
            P("dp", "col", "row"),
            P("dp", "col", "row"),
            P("row", "col"),
            P("row", "col"),
        ),
        check_vma=False,
    )
```

profile of v0, /device:TPU:0, one launch (start us, length us, event | category | flops | bytes accessed | tf_op | source)
XLA Modules:
  0.0 593.3 jit_solution(1535676170303104737)
XLA Ops:
  7.9 1.9 copy.22
  9.9 30.9 %all-gather.7.cloned.1.call-done = bf16[1,512,3072]{2,1,0:T(8,128)(2,1)} async-done(((bf16[1,128,3072]{2,1,0:T(8,128)(2,1)}), bf16[1,512,3072]{2,1,0:T(8,128)(2,1)}) %all-gather.7.cloned.1.call-update) | async-done | bytes 3145744 | tf_op jit(solution)/shard_map/all_gather | solution.py:39
  40.8 10.6 %fusion.2 = f32[512,1536]{1,0:T(8,128)} fusion(bf16[1536,3072]{1,0:T(8,128)(2,1)} %param.10, bf16[1,512,3072]{2,1,0:T(8,128)(2,1)} %all-gather.7.cloned.1.call-done), kind=kOutput, calls=%fused_computation.4 | convolution fusion | flops 4831838208 | bytes 15728640 | tf_op jit(solution)/shard_map/dot_general | solution.py:41
  53.7 27.0 %all-gather.5.cloned.1.call-done = bf16[1,512,1536]{1,2,0:T(8,128)(2,1)} async-done(((bf16[1,128,1536]{1,2,0:T(8,128)(2,1)}), bf16[1,512,1536]{1,2,0:T(8,128)(2,1)}) %all-gather.5.cloned.1.call-update) | async-done | bytes 1572880 | tf_op jit(solution)/shard_map/all_gather | solution.py:21
  80.7 2.1 multiply_reduce_fusion
  84.4 57.7 %reduce-scatter.4.cloned.1.call-done = f32[128,1536]{1,0:T(8,128)} async-done(((f32[512,1536]{1,0:T(8,128)}), f32[128,1536]{1,0:T(8,128)}) %reduce-scatter.4.cloned.1.call-update) | async-done | bytes 786448 | tf_op jit(solution)/shard_map/reduce_scatter | solution.py:40
  143.5 38.4 %all-gather.9.cloned.1.call-done = bf16[1,512,1536]{1,2,0:T(8,128)(2,1)} async-done(((bf16[1,128,1536]{1,2,0:T(8,128)(2,1)}), bf16[1,512,1536]{1,2,0:T(8,128)(2,1)}) %all-gather.9.cloned.1.call-update) | async-done | bytes 1572880 | tf_op jit(solution)/shard_map/all_gather | solution.py:22
  181.9 2.7 multiply_reduce_fusion.1
  184.7 2.0 multiply_convert_fusion.1
  186.7 2.7 multiply_convert_fusion
  189.4 2.7 copy.29
  193.8 2.6 copy.30
  196.6 20.1 %all_gather.19 = bf16[1,512,364]{1,2,0:T(8,128)(2,1)S(1)} all-gather(bf16[1,128,364]{1,2,0:T(8,128)(2,1)S(1)} %copy-done.5), channel_id=1, replica_groups=mesh['dp'=2,'row'=4,'col'=4] {'col'}, dimensions={1}, use_global_device_ids=true | all-gather | bytes 465920 | tf_op jit(solution)/shard_map/all_gather | solution.py:23
  216.7 4.6 convolution_convert_fusion.1
  221.3 5.5 all-gather.11.cloned.1.call-done
  226.8 9.3 %convolution_convert_fusion = bf16[1536,3072]{1,0:T(8,128)(2,1)} fusion(bf16[1,512,3072]{2,1,0:T(8,128)(2,1)} %all-gather.7.cloned.1.call-done, bf16[1,512,1536]{1,2,0:T(8,128)(2,1)} %all-gather.11.cloned.1.call-done), kind=kOutput, calls=%fused_computation | convolution fusion | flops 4836556800 | bytes 14155776 | tf_op jit(solution)/shard_map/dot_general | solution.py:10
  238.9 2.3 copy.31
  241.2 21.2 %reduce-scatter.6.cloned.1.call-done = bf16[128,1536]{1,0:T(8,128)(2,1)} async-done(((bf16[512,1536]{1,0:T(8,128)(2,1)}), bf16[128,1536]{1,0:T(8,128)(2,1)}) %reduce-scatter.6.cloned.1.call-update) | async-done | bytes 393232 | tf_op jit(solution)/shard_map/reduce_scatter | solution.py:69
  262.4 2.0 bitcast_convert_fusion.1
  264.4 34.6 %reduce-scatter.8.cloned.1.call-done = bf16[128,1536]{1,0:T(8,128)(2,1)} async-done(((bf16[512,1536]{1,0:T(8,128)(2,1)}), bf16[128,1536]{1,0:T(8,128)(2,1)}) %reduce-scatter.8.cloned.1.call-update) | async-done | bytes 393232 | tf_op jit(solution)/shard_map/reduce_scatter | solution.py:75
  299.0 2.0 bitcast_convert_fusion
  301.0 270.0 %all-reduce.3.cloned.1.call-done = (bf16[1536,3072]{1,0:T(8,128)(2,1)}, bf16[364,3072]{1,0:T(8,128)(2,1)}) async-done(((bf16[1536,3072]{1,0:T(8,128)(2,1)}, bf16[364,3072]{1,0:T(8,128)(2,1)}), (bf16[1536,3072]{1,0:T(8,128)(2,1)}, bf16[364,3072]{1,0:T(8,128)(2,1)})) %all-reduce.3.cloned.1.call-update) | async-done | bytes 11673616 | tf_op jit(solution)/shard_map/psum | solution.py:85
  571.0 12.9 %convert_element_type.71 = f32[1536,3072]{1,0:T(8,128)} convert(bf16[1536,3072]{1,0:T(8,128)(2,1)} %get-tuple-element.15) | non-fusion elementwise | flops 4718592 | bytes 28311552 | tf_op jit(solution)/shard_map/convert_element_type | solution.py:85
  583.8 2.7 convert_element_type.73
  (37 shorter events, 10.7 us)
Async XLA Ops:
  7.2 33.7 %all-gather.7.cloned.1.call-start = ((), (), s32[]{:S(2)}) async-start(), calls=%async_computation.4 | async-start | bytes 3932160 | tf_op jit(solution)/shard_map/all_gather | solution.py:39
  7.9 72.8 %all-gather.5.cloned.1.call-start = ((), (), s32[]{:S(2)}) async-start(), calls=%async_computation.3 | async-start | bytes 1966080 | tf_op jit(solution)/shard_map/all_gather | solution.py:21
  9.9 132.2 %reduce-scatter.4.cloned.1.call-start = ((), (), s32[]{:S(2)}) async-start(), calls=%async_computation.5 | async-start | bytes 3932160 | tf_op jit(solution)/shard_map/reduce_scatter | solution.py:40
  51.4 1.0 copy-start.3
  51.4 2.0 copy-start.4
  51.4 130.4 %all-gather.9.cloned.1.call-start = ((), (), s32[]{:S(2)}) async-start(), calls=%async_computation.6 | async-start | bytes 1966080 | tf_op jit(solution)/shard_map/all_gather | solution.py:22
  53.4 173.4 %all-gather.11.cloned.1.call-start = ((), (), s32[]{:S(2)}) async-start(), calls=%async_computation.9 | async-start | bytes 1966080 | tf_op jit(solution)/shard_map/all_gather | solution.py:60
  53.6 30.2 %copy-start.1 = (bf16[1,128,1536]{1,2,0:T(8,128)(2,1)}, bf16[1,128,1536]{1,2,0:T(8,128)(2,1)S(1)}, u32[]{:S(2)}) copy-start(bf16[1,128,1536]{1,2,0:T(8,128)(2,1)S(1)} %copy.21) | copy-start | bytes 1179652
  184.6 77.8 %reduce-scatter.6.cloned.1.call-start = ((), (), s32[]{:S(2)}) async-start(), calls=%async_computation.7 | async-start | bytes 1966080 | tf_op jit(solution)/shard_map/reduce_scatter | solution.py:69
  192.1 106.9 %reduce-scatter.8.cloned.1.call-start = ((), (), s32[]{:S(2)}) async-start(), calls=%async_computation.8 | async-start | bytes 1966080 | tf_op jit(solution)/shard_map/reduce_scatter | solution.py:75
  193.8 2.7 copy-start.5
  196.5 374.5 %all-reduce.3.cloned.1.call-start = ((), (), s32[]{:S(2)}) async-start(), calls=%async_computation.10 | async-start | bytes 23396352 | tf_op jit(solution)/shard_map/psum | solution.py:85
  236.1 1.4 copy-start
  571.0 12.9 %copy-start.2 = (bf16[364,3072]{1,0:T(8,128)(2,1)S(1)}, bf16[364,3072]{1,0:T(8,128)(2,1)}, u32[]{:S(2)}) copy-start(bf16[364,3072]{1,0:T(8,128)(2,1)} %get-tuple-element.16) | copy-start | bytes 6709252
Sparse Core Ops, SparseCore 0:
  9.6 31.2 all-gather.6
  43.0 37.7 all-gather.4
  83.6 58.4 reduce-scatter.3
  144.1 37.7 all-gather.8
  184.7 41.9 all-gather.10
  228.9 33.4 reduce-scatter.5
  264.7 34.2 reduce-scatter.7
  302.1 268.8 all-reduce.2
where the time goes:
time: 594 us; the launch traced here: 593 us
  waiting for transfers between devices  486 us (82%)
  matrix products  37.2 us (6%)
  other arithmetic  22.1 us (4%)
  blocking collectives  20.1 us (3%)
  between operations  14.2 us (2%)
  local copies, waits for them, and re-layouts  13.2 us (2%)
    psum x1, waiting for transfers between devices, body(): lax.psum(out_part.astype(jnp.bfloat16), 'dp').astype(jnp.float32)  270 us
    reduce_scatter x1, waiting for transfers between devices, body(): lax.psum_scatter(lax.dot_general(dense_grad, out_weight, (((1,), (1,)), (...  57.7 us
    all_gather x1, waiting for transfers between devices, body(): lax.all_gather(attn_values, 'col', axis=1, tiled=True)  38.4 us
    reduce_scatter x1, waiting for transfers between devices, body(): lax.psum_scatter(value_term.reshape(-1, feature_width).astype(jnp.bfloat1...  34.6 us
    all_gather x1, waiting for transfers between devices, body(): dense_grad = lax.all_gather(output_grad, 'row', axis=1, tiled=True)[0]  30.9 us
    all_gather x1, waiting for transfers between devices, body(): lax.all_gather(attn_keys, 'col', axis=1, tiled=True)  27 us
    reduce_scatter x1, waiting for transfers between devices, body(): lax.psum_scatter(key_term.reshape(-1, feature_width).astype(jnp.bfloat16)...  21.2 us
    all_gather x1, blocking collectives, body(): lax.all_gather(patches, 'col', axis=1, tiled=True)  20.1 us
  transfers between devices with their start and end apart: 8, of which 8 were waited for; matrix products, arithmetic and copies ran while one was open for 9% of the time, Pallas kernels for 0%

commit v1 on v0

--- a/solution.py
+++ b/solution.py
@@ -4,6 +4,11 @@
 from jax.sharding import PartitionSpec as P
 
 DH = 128
+
+
+def summed_here(array, mesh_axis):
+    pieces = lax.all_gather(array, mesh_axis)
+    return jnp.sum(pieces, axis=0)
 
 
 def contract_rows(left, right):
@@ -82,7 +87,7 @@
     out_part = contract_rows(every_out[0], dense_grad)
     embed_part = contract_rows(every_patch[0], dense_grad)
     out_weight_grad, embed_weight_grad = (
-        lax.psum(out_part.astype(jnp.bfloat16), "dp").astype(jnp.float32),
+        summed_here(out_part.astype(jnp.bfloat16), "dp").astype(jnp.float32),
         lax.psum(embed_part.astype(jnp.bfloat16), "dp").astype(jnp.float32),
     )
     return (

time: 594 us -> 628 us (1.057)
  waiting for transfers between devices: 486 us -> 507 us
  other arithmetic: 22.1 us -> 40.5 us
    all_gather x0 -> x1, waiting for transfers between devices: none -> 224 us  [summed_here(): pieces = lax.all_gather(array, mesh_axis)]
    psum x1, waiting for transfers between devices: 270 us -> 60.1 us  [body(): lax.psum(embed_part.astype(jnp.bfloat16), 'dp').astype(jnp.float32)]
    reduce_sum x0 -> x1, other arithmetic: none -> 16.8 us  [summed_here(): return jnp.sum(pieces, axis=0)]
    reduce_scatter x1, waiting for transfers between devices: 21.2 us -> 29.6 us  [body(): lax.psum_scatter(key_term.reshape(-1, feature_width).astype(jnp.bfloat16)...]
  transfers between devices with their start and end apart: 8 -> 9, of which waited for: 8 -> 9; matrix products, arithmetic and copies ran while one was open for 9% -> 9% of each run, Pallas kernels for 0% -> 0%
where the time goes in v1:
time: 628 us; the launch traced here: 627 us
  waiting for transfers between devices  507 us (81%)
  other arithmetic  40.5 us (6%)
  matrix products  37.4 us (6%)
  blocking collectives  16.3 us (3%)
  between operations  13.9 us (2%)
  local copies, waits for them, and re-layouts  11.8 us (2%)
    all_gather x1, waiting for transfers between devices, summed_here(): pieces = lax.all_gather(array, mesh_axis)  224 us
    psum x1, waiting for transfers between devices, body(): lax.psum(embed_part.astype(jnp.bfloat16), 'dp').astype(jnp.float32)  60.1 us
    reduce_scatter x1, waiting for transfers between devices, body(): lax.psum_scatter(lax.dot_general(dense_grad, out_weight, (((1,), (1,)), (...  57.7 us
    all_gather x1, waiting for transfers between devices, body(): lax.all_gather(attn_values, 'col', axis=1, tiled=True)  38.4 us
    reduce_scatter x1, waiting for transfers between devices, body(): lax.psum_scatter(value_term.reshape(-1, feature_width).astype(jnp.bfloat1...  34.7 us
    all_gather x1, waiting for transfers between devices, body(): dense_grad = lax.all_gather(output_grad, 'row', axis=1, tiled=True)[0]  30.9 us
    reduce_scatter x1, waiting for transfers between devices, body(): lax.psum_scatter(key_term.reshape(-1, feature_width).astype(jnp.bfloat16)...  29.6 us
    all_gather x1, waiting for transfers between devices, body(): lax.all_gather(attn_keys, 'col', axis=1, tiled=True)  27 us
  transfers between devices with their start and end apart: 9, of which 9 were waited for; matrix products, arithmetic and copies ran while one was open for 9% of the time, Pallas kernels for 0%

profile of v1, /device:TPU:0, one launch (start us, length us, event | category | flops | bytes accessed | tf_op | source)
XLA Modules:
  0.0 627.1 jit_solution(8002021358424501275)
XLA Ops:
  9.9 30.9 %all-gather.9.cloned.1.call-done = bf16[1,512,3072]{2,1,0:T(8,128)(2,1)} async-done(((bf16[1,128,3072]{2,1,0:T(8,128)(2,1)}), bf16[1,512,3072]{2,1,0:T(8,128)(2,1)}) %all-gather.9.cloned.1.call-update) | async-done | bytes 3145744 | tf_op jit(solution)/shard_map/all_gather | solution.py:44
  40.8 10.6 %fusion.2 = f32[512,1536]{1,0:T(8,128)} fusion(bf16[1536,3072]{1,0:T(8,128)(2,1)} %param.10, bf16[1,512,3072]{2,1,0:T(8,128)(2,1)} %all-gather.9.cloned.1.call-done), kind=kOutput, calls=%fused_computation.4 | convolution fusion | flops 4831838208 | bytes 15728640 | tf_op jit(solution)/shard_map/dot_general | solution.py:46
  53.7 27.0 %all-gather.7.cloned.1.call-done = bf16[1,512,1536]{1,2,0:T(8,128)(2,1)} async-done(((bf16[1,128,1536]{1,2,0:T(8,128)(2,1)}), bf16[1,512,1536]{1,2,0:T(8,128)(2,1)}) %all-gather.7.cloned.1.call-update) | async-done | bytes 1572880 | tf_op jit(solution)/shard_map/all_gather | solution.py:26
  80.7 2.1 multiply_reduce_fusion
  84.4 57.7 %reduce-scatter.4.cloned.1.call-done = f32[128,1536]{1,0:T(8,128)} async-done(((f32[512,1536]{1,0:T(8,128)}), f32[128,1536]{1,0:T(8,128)}) %reduce-scatter.4.cloned.1.call-update) | async-done | bytes 786448 | tf_op jit(solution)/shard_map/reduce_scatter | solution.py:45
  143.5 38.4 %all-gather.11.cloned.1.call-done = bf16[1,512,1536]{1,2,0:T(8,128)(2,1)} async-done(((bf16[1,128,1536]{1,2,0:T(8,128)(2,1)}), bf16[1,512,1536]{1,2,0:T(8,128)(2,1)}) %all-gather.11.cloned.1.call-update) | async-done | bytes 1572880 | tf_op jit(solution)/shard_map/all_gather | solution.py:27
  181.9 2.7 multiply_reduce_fusion.1
  184.7 16.3 %all_gather.27 = bf16[1,512,364]{1,2,0:T(8,128)(2,1)S(1)} all-gather(bf16[1,128,364]{1,2,0:T(8,128)(2,1)S(1)} %copy-done.4), channel_id=1, replica_groups=mesh['dp'=2,'row'=4,'col'=4] {'col'}, dimensions={1}, use_global_device_ids=true | all-gather | bytes 465920 | tf_op jit(solution)/shard_map/all_gather | solution.py:28
  200.9 4.6 convolution_convert_fusion.1
  205.7 2.1 multiply_convert_fusion.1
  207.7 2.7 multiply_convert_fusion
  210.4 2.6 copy.29
  214.8 2.7 copy.30
  217.7 4.0 all-gather.13.cloned.1.call-done
  221.7 9.5 %convolution_convert_fusion = bf16[1536,3072]{1,0:T(8,128)(2,1)} fusion(bf16[1,512,3072]{2,1,0:T(8,128)(2,1)} %all-gather.9.cloned.1.call-done, bf16[1,512,1536]{1,2,0:T(8,128)(2,1)} %all-gather.13.cloned.1.call-done), kind=kOutput, calls=%fused_computation | convolution fusion | flops 4836556800 | bytes 14155776 | tf_op jit(solution)/shard_map/dot_general | solution.py:15
  231.2 60.1 %all-reduce.2.cloned.1.call-done = bf16[364,3072]{1,0:T(8,128)(2,1)} async-done(((bf16[364,3072]{1,0:T(8,128)(2,1)}), bf16[364,3072]{1,0:T(8,128)(2,1)}) %all-reduce.2.cloned.1.call-update) | async-done | bytes 2236432 | tf_op jit(solution)/shard_map/psum | solution.py:91
  291.3 4.3 convert_element_type.75
  297.1 2.3 copy.31
  299.4 29.6 %reduce-scatter.6.cloned.1.call-done = bf16[128,1536]{1,0:T(8,128)(2,1)} async-done(((bf16[512,1536]{1,0:T(8,128)(2,1)}), bf16[128,1536]{1,0:T(8,128)(2,1)}) %reduce-scatter.6.cloned.1.call-update) | async-done | bytes 393232 | tf_op jit(solution)/shard_map/reduce_scatter | solution.py:74
  328.9 2.0 bitcast_convert_fusion.1
  330.9 34.7 %reduce-scatter.8.cloned.1.call-done = bf16[128,1536]{1,0:T(8,128)(2,1)} async-done(((bf16[512,1536]{1,0:T(8,128)(2,1)}), bf16[128,1536]{1,0:T(8,128)(2,1)}) %reduce-scatter.8.cloned.1.call-update) | async-done | bytes 393232 | tf_op jit(solution)/shard_map/reduce_scatter | solution.py:80
  367.5 223.5 %all-gather.15.cloned.1.call-done = bf16[3072,3072]{1,0:T(8,128)(2,1)} async-done(((bf16[1536,3072]{1,0:T(8,128)(2,1)}), bf16[3072,3072]{1,0:T(8,128)(2,1)}) %all-gather.15.cloned.1.call-update) | async-done | bytes 18874384 | tf_op jit(solution)/shard_map/all_gather | solution.py:10
  591.1 16.8 %reduce_sum.32 = bf16[1536,3072]{1,0:T(8,128)(2,1)} reduce(bf16[2,1536,3072]{2,1,0:T(8,128)(2,1)} %bitcast.51, bf16[]{:T(256)} %constant.3.clone.1), dimensions={0}, to_apply=%region_6.0 | reduce | flops 4718592 | bytes 28311554 | tf_op jit(solution)/shard_map/reduce_sum | solution.py:11
  607.9 12.8 %convert_element_type.73 = f32[1536,3072]{1,0:T(8,128)} convert(bf16[1536,3072]{1,0:T(8,128)(2,1)} %reduce_sum.32) | non-fusion elementwise | flops 4718592 | bytes 28311552 | tf_op jit(solution)/shard_map/convert_element_type | solution.py:90
  (39 shorter events, 13.4 us)
Async XLA Ops:
  7.2 33.7 %all-gather.9.cloned.1.call-start = ((), (), s32[]{:S(2)}) async-start(), calls=%async_computation.4 | async-start | bytes 3932160 | tf_op jit(solution)/shard_map/all_gather | solution.py:44
  7.9 72.8 %all-gather.7.cloned.1.call-start = ((), (), s32[]{:S(2)}) async-start(), calls=%async_computation.3 | async-start | bytes 1966080 | tf_op jit(solution)/shard_map/all_gather | solution.py:26
  9.9 132.2 %reduce-scatter.4.cloned.1.call-start = ((), (), s32[]{:S(2)}) async-start(), calls=%async_computation.5 | async-start | bytes 3932160 | tf_op jit(solution)/shard_map/reduce_scatter | solution.py:45
  51.4 1.0 copy-start.2
  51.4 2.0 copy-start.3
  51.4 130.4 %all-gather.11.cloned.1.call-start = ((), (), s32[]{:S(2)}) async-start(), calls=%async_computation.6 | async-start | bytes 1966080 | tf_op jit(solution)/shard_map/all_gather | solution.py:27
  53.4 168.4 %all-gather.13.cloned.1.call-start = ((), (), s32[]{:S(2)}) async-start(), calls=%async_computation.9 | async-start | bytes 1966080 | tf_op jit(solution)/shard_map/all_gather | solution.py:65
  53.6 30.2 %copy-start.1 = (bf16[1,128,1536]{1,2,0:T(8,128)(2,1)}, bf16[1,128,1536]{1,2,0:T(8,128)(2,1)S(1)}, u32[]{:S(2)}) copy-start(bf16[1,128,1536]{1,2,0:T(8,128)(2,1)S(1)} %copy.21) | copy-start | bytes 1179652
  84.4 100.3 %copy-start.4 = (bf16[1,128,364]{1,2,0:T(8,128)(2,1)S(1)}, bf16[1,128,364]{1,2,0:T(8,128)(2,1)}, u32[]{:S(2)}) copy-start(bf16[1,128,364]{1,2,0:T(8,128)(2,1)} %param.6) | copy-start | bytes 279556
  184.6 106.7 %all-reduce.2.cloned.1.call-start = ((), (), s32[]{:S(2)}) async-start(), calls=%async_computation.10 | async-start | bytes 4521984 | tf_op jit(solution)/shard_map/psum | solution.py:91
  205.6 123.3 %reduce-scatter.6.cloned.1.call-start = ((), (), s32[]{:S(2)}) async-start(), calls=%async_computation.7 | async-start | bytes 1966080 | tf_op jit(solution)/shard_map/reduce_scatter | solution.py:74
  213.0 152.5 %reduce-scatter.8.cloned.1.call-start = ((), (), s32[]{:S(2)}) async-start(), calls=%async_computation.8 | async-start | bytes 1966080 | tf_op jit(solution)/shard_map/reduce_scatter | solution.py:80
  217.5 373.6 %all-gather.15.cloned.1.call-start = ((), (), s32[]{:S(2)}) async-start(), calls=%async_computation.11 | async-start | bytes 28311552 | tf_op jit(solution)/shard_map/all_gather | solution.py:10
  231.2 64.4 %copy-start = (bf16[1,512,1536]{1,2,0:T(8,128)(2,1)S(1)}, bf16[1,512,1536]{1,2,0:T(8,128)(2,1)}, u32[]{:S(2)}) copy-start(bf16[1,512,1536]{1,2,0:T(8,128)(2,1)} %all-gather.7.cloned.1.call-done) | copy-start | bytes 4718596
Sparse Core Ops, SparseCore 0:
  9.6 31.2 all-gather.8
  43.0 37.7 all-gather.6
  83.6 58.4 reduce-scatter.3
  144.1 37.7 all-gather.10
  184.7 36.9 all-gather.12
  224.4 66.8 all-reduce.1
  293.6 35.2 reduce-scatter.5
  331.2 34.2 reduce-scatter.7
  367.7 223.3 all-gather.14
